TPU v7x, 32 devices: a whole 2x2x4 slice. The times are simulated.
32 devices in a mesh: inner: 2 (over y), outer: 16 (over z, x, core).
Axes of the slice: x: 2, y: 2, z: 4, core: 2. Of those that a mesh axis runs over, the one named last changes fastest.
Arguments:
- propagator_matrices: bfloat16 [16, 48, 256, 256], P('outer', 'inner')
- smoothed_adjoints: float32 [16, 48, 256], P('outer', 'inner'), may hold values from -0.4330127 to 0.4330127
- station_loadings: float32 [16, 48, 2, 128], P('outer', 'inner'), may hold values from -0.21650635 to 0.21650635
- offset_response: float32 [16, 48, 256], P('outer', 'inner'), may hold values from -0.021650635 to 0.021650635
Outputs:
- adjoint: float32 [16, 48, 256], P('outer', 'inner')
- spatial_matrix_derivative: float32 [128, 128], replicated
- variance_derivative: float32 [], replicated
All inputs are finite; a program needn't handle non-finite values.
Results may differ from a plain program's by a relative error of at most 0.0003.
Values sent between devices are 32-bit elements; how exact they have to be, the bound alone decides.
No kernel may reach another device: no remote copies, remote signals or barrier semaphores. Data moves between devices by JAX's collectives and lax.ppermute only.
A program may use at most 128 MiB of HBM per device.

v0:
```python
import jax
import jax.numpy as jnp
from jax import lax
from jax.sharding import PartitionSpec as P


def entering(value, axis, join, neutral):
    count, mine = (lax.axis_size(axis), lax.axis_index(axis))
    pieces = jax.tree.map(lambda part: lax.all_gather(part, axis), value)
    pieces = jax.tree.map(lambda part: part[::-1], pieces)
    mine = count - 1 - mine
    subtotal = jax.tree.map(
        lambda part, zero: jnp.full_like(part, 0) + jnp.asarray(zero, part.dtype), value, neutral
    )

    def turn(position, subtotal):
        longer = join(subtotal, jax.tree.map(lambda part: part[position], pieces))
        return jax.tree.map(lambda new, old: jnp.where(position < mine, new, old), longer, subtotal)

    return lax.fori_loop(0, count - 1, turn, subtotal)


def spread(block, axis, source):
    block = jnp.where(lax.axis_index(axis) == source, block, jnp.zeros_like(block))
    return lax.psum(block, axis)


def compose(earlier, later):
    return (
        jnp.dot(later[0], earlier[0], precision=lax.Precision.HIGHEST),
        jnp.dot(later[0], earlier[1], precision=lax.Precision.HIGHEST) + later[1],
    )


def body(propagator_matrices, smoothed_adjoints, station_loadings, offset_response):
    blocks = propagator_matrices[0]
    derivative_results = smoothed_adjoints[0]
    width = derivative_results.shape[1]
    stations = station_loadings.shape[3]
    unit = jnp.eye(width, dtype=jnp.float32)
    nothing = jnp.zeros((width,), jnp.float32)

    def summarize(carry, items):
        matrix, grad_row = items
        wide = matrix.astype(jnp.float32)
        new_mat = jnp.dot(wide.T, carry[0], precision=lax.Precision.HIGHEST)
        new_vec = jnp.dot(grad_row + carry[1], wide, precision=lax.Precision.HIGHEST)
        return ((new_mat, new_vec), None)

    (own_mat, own_vec), _ = lax.scan(
        summarize, (unit, nothing), (blocks, derivative_results), reverse=True
    )
    suf_mat, suf_vec = entering((own_mat, own_vec), "inner", compose, (unit, nothing))
    whole_mat, whole_vec = compose((suf_mat, suf_vec), (own_mat, own_vec))
    packed = jnp.concatenate([whole_mat, whole_vec[None, :]], axis=0)
    shared = spread(packed, "inner", 0)
    total_mat = shared[:width]
    total_vec = shared[width]
    beyond_mat, beyond_vec = entering((total_mat, total_vec), "outer", compose, (unit, nothing))
    incoming = jnp.dot(suf_mat, beyond_vec, precision=lax.Precision.HIGHEST) + suf_vec

    def backward(carry, items):
        matrix, grad_row = items
        lam = grad_row + carry
        message = jnp.dot(lam, matrix.astype(jnp.float32), precision=lax.Precision.HIGHEST)
        return (message, lam)

    _, length_rates = lax.scan(backward, incoming, (blocks, derivative_results), reverse=True)
    argument_values = station_loadings[0]
    local_kernel = jnp.dot(
        length_rates[:, :stations].T, argument_values[:, 0, :], precision=lax.Precision.HIGHEST
    )
    local_kernel = local_kernel + jnp.dot(
        length_rates[:, stations:].T, argument_values[:, 1, :], precision=lax.Precision.HIGHEST
    )
    local_noise = -jnp.sum(length_rates * offset_response[0])
    spatial_matrix_derivative, variance_derivative = lax.psum(
        (local_kernel, local_noise), ("inner", "outer")
    )
    return (length_rates[None], spatial_matrix_derivative, variance_derivative)


def solution(mesh):
    return jax.shard_map(
        body,
        mesh=mesh,
        in_specs=(
            P("outer", "inner", None, None),
            P("outer", "inner", None),
            P("outer", "inner", None, None),
            P("outer", "inner", None),
        ),
        out_specs=(P("outer", "inner", None), P(), P()),
        check_vma=False,
    )
```

profile of v0, /device:TPU:1, one launch (start us, length us, event | category | flops | bytes accessed | tf_op | source)
XLA Modules:
  0.0 369.9 jit_solution(7613051268337838645)
XLA Ops:
  7.3 73.5 %while.52 = (s32[]{:T(128)}, f32[256,256]{1,0:T(8,128)S(1)}, f32[256]{0:T(256)S(1)}, bf16[24,256,256]{2,1,0:T(8,128)(2,1)}, f32[24,256]{1,0:T(8,128)}, /*index=5*/s32[]{:T(128)}, s32[]{:T(128)}) while((s32[]{:T(128)}, f32[256,256]{1,0:T(8,128)S(1)}, f32[256]{0:T(256)S(1)}, bf16[24,256,256]{2,1,0:T(8,128)(2,1)}, f32[24,256]{1,0:T(8,128)}, ...), condition=%wide.region_1.2_spmd, body=%wide.region_0.1_spmd.sunk | while | flops 202113280 | bytes 1317989 | solution.py:50
  8.0 1.0 fusion.59
  9.1 1.3 fusion.58
  11.1 1.0 fusion.59
  12.1 1.3 fusion.58
  14.1 1.0 fusion.59
  15.2 1.3 fusion.58
  17.2 1.0 fusion.59
  18.2 1.3 fusion.58
  20.3 1.0 fusion.59
  21.3 1.3 fusion.58
  23.3 1.0 fusion.59
  24.4 1.3 fusion.58
  26.4 1.0 fusion.59
  27.4 1.3 fusion.58
  30.5 1.3 fusion.58
  32.5 1.0 fusion.59
  33.6 1.3 fusion.58
  35.6 1.0 fusion.59
  36.6 1.3 fusion.58
  39.7 1.3 fusion.58
  41.7 1.0 fusion.59
  42.7 1.3 fusion.58
  44.8 1.0 fusion.59
  45.8 1.3 fusion.58
  48.9 1.3 fusion.58
  50.9 1.0 fusion.59
  51.9 1.3 fusion.58
  55.0 1.3 fusion.58
  58.1 1.3 fusion.58
  61.1 1.3 fusion.58
  64.2 1.3 fusion.58
  67.3 1.3 fusion.58
  70.3 1.3 fusion.58
  73.4 1.3 fusion.58
  76.4 1.3 fusion.58
  79.5 1.3 fusion.58
  80.8 3.7 all-gather.3
  84.5 6.9 %all-gather = f32[512,256]{1,0:T(8,128)S(1)} all-gather(f32[256,256]{1,0:T(8,128)S(1)} %get-tuple-element.325), channel_id=2, replica_groups=mesh['inner'=2,'outer'=16] {'inner'}, dimensions={0}, use_global_device_ids=true | all-gather | bytes 786432 | tf_op jit(solution)/shard_map/all_gather | solution.py:9
  93.6 26.5 %all-reduce.3.cloned.1.call-done = f32[257,256]{1,0:T(8,128)} async-done(((f32[257,256]{1,0:T(8,128)}), f32[257,256]{1,0:T(8,128)}) %all-reduce.3.cloned.1.call-update) | async-done | bytes 263184 | tf_op jit(solution)/shard_map/psum | solution.py:25
  120.1 1.7 slice.33
  122.6 22.0 %all-gather.4 = f32[16,1,256]{2,1,0:T(1,128)S(1)} all-gather(f32[1,1,256]{2,1,0:T(1,128)S(1)} %slice_bitcast_fusion), channel_id=1, replica_groups=mesh['inner'=2,'outer'=16] {'outer'}, dimensions={0}, use_global_device_ids=true | all-gather | bytes 17408 | tf_op jit(solution)/shard_map/all_gather | solution.py:9
  144.6 29.2 %all-gather.7.cloned.1.call-done = f32[4096,256]{1,0:T(8,128)} async-done(((f32[256,256]{1,0:T(8,128)}), f32[4096,256]{1,0:T(8,128)}) %all-gather.7.cloned.1.call-update) | async-done | bytes 4194320 | tf_op jit(solution)/shard_map/all_gather | solution.py:9
  173.8 4.6 %rev.8 = f32[16,256,256]{2,1,0:T(8,128)} reverse(f32[16,256,256]{2,1,0:T(8,128)} %bitcast.93), dimensions={0} | reverse | bytes 8388608 | tf_op jit(solution)/shard_map/rev | solution.py:10
  178.4 20.1 %while.54 = (s32[]{:T(128)}, f32[256]{0:T(256)S(1)}, s32[]{:T(128)}, f32[16,256,256]{2,1,0:T(8,128)}, f32[16,256]{1,0:T(8,128)S(1)}, /*index=5*/s32[]{:T(128)}, s32[]{:T(128)}) while((s32[]{:T(128)}, f32[256]{0:T(256)S(1)}, s32[]{:T(128)}, f32[16,256,256]{2,1,0:T(8,128)}, f32[16,256]{1,0:T(8,128)S(1)}, /*index=5*/s32[]{:T(128)}, ...), condition=%wide.region_4.5_spmd.clone, body=%wide.region_3.4_spmd.clone.sunk | while | flops 787460 | bytes 272498 | solution.py:20
  178.4 1.2 fusion.65
  179.7 1.2 fusion.65
  181.1 1.2 fusion.65
  182.4 1.2 fusion.65
  183.7 1.2 fusion.65
  185.1 1.2 fusion.65
  186.4 1.2 fusion.65
  187.8 1.2 fusion.65
  189.1 1.2 fusion.65
  190.5 1.2 fusion.65
  191.8 1.2 fusion.65
  193.2 1.2 fusion.65
  194.5 1.2 fusion.65
  195.9 1.2 fusion.65
  197.2 1.2 fusion.65
  198.8 44.2 %while.53 = (s32[]{:T(128)}, f32[256]{0:T(256)S(1)}, f32[24,256]{1,0:T(8,128)S(1)}, f32[24,256]{1,0:T(8,128)}, bf16[24,256,256]{2,1,0:T(8,128)(2,1)}, /*index=5*/s32[]{:T(128)}, s32[]{:T(128)}, s32[]{:T(128)}) while((s32[]{:T(128)}, f32[256]{0:T(256)S(1)}, f32[24,256]{1,0:T(8,128)S(1)}, f32[24,256]{1,0:T(8,128)}, ...), condition=%wide.region_6.7_spmd, body=%wide.region_5.6_spmd.sunk | while | flops 786691 | bytes 140397 | solution.py:68
  245.6 38.7 %psum.23 = f32[]{:T(128)} all-reduce(f32[]{:T(128)S(6)} %neg.3), channel_id=1, replica_groups=mesh['inner'=2,'outer'=16] {'inner','outer'}, use_global_device_ids=true, to_apply=%region_9.10 | all-reduce | flops 1 | bytes 8 | tf_op jit(solution)/shard_map/psum | solution.py:77
  284.2 77.7 %all-reduce.5.cloned.1.call-done = f32[128,128]{1,0:T(8,128)} async-done(((f32[128,128]{1,0:T(8,128)}), f32[128,128]{1,0:T(8,128)}) %all-reduce.5.cloned.1.call-update) | async-done | bytes 65552 | tf_op jit(solution)/shard_map/psum | solution.py:77
  361.9 1.5 copy.39
  (258 shorter events, 80.0 us)
Async XLA Ops:
  7.2 112.9 %all-reduce.3.cloned.1.call-start = ((), (), s32[]{:S(2)}) async-start(), calls=%async_computation | async-start | bytes 540672 | tf_op jit(solution)/shard_map/psum | solution.py:25
  80.8 41.1 %copy-start.1 = (f32[1,24,2,128]{3,2,1,0:T(2,128)S(1)}, f32[1,24,2,128]{3,2,1,0:T(2,128)}, u32[]{:S(2)}) copy-start(f32[1,24,2,128]{3,2,1,0:T(2,128)} %param.12) | copy-start | bytes 73732
  93.5 80.3 %all-gather.7.cloned.1.call-start = ((), (), s32[]{:S(2)}) async-start(), calls=%async_computation.2 | async-start | bytes 4456448 | tf_op jit(solution)/shard_map/all_gather | solution.py:9
  121.8 240.1 %all-reduce.5.cloned.1.call-start = ((), (), s32[]{:S(2)}) async-start(), calls=%async_computation.1 | async-start | bytes 131072 | tf_op jit(solution)/shard_map/psum | solution.py:77
  173.8 70.5 %copy-start.2 = (f32[1,24,256]{2,1,0:T(8,128)S(1)}, f32[1,24,256]{2,1,0:T(8,128)}, u32[]{:S(2)}) copy-start(f32[1,24,256]{2,1,0:T(8,128)} %param.13) | copy-start | bytes 73732
  243.0 120.3 %copy-start = (f32[24,256]{1,0:T(8,128)}, f32[24,256]{1,0:T(8,128)S(1)}, u32[]{:S(2)}) copy-start(f32[24,256]{1,0:T(8,128)S(1)} %get-tuple-element.328) | copy-start | bytes 73732
Sparse Core Ops, SparseCore 0:
  93.6 26.3 all-reduce.2
  122.5 51.2 all-gather.6
  244.4 117.4 all-reduce.4
where the time goes:
time: 374 us; the launch traced here: 370 us
  waiting for transfers between devices  133 us (36%)
  matrix products  101 us (27%)
  blocking collectives  71.3 us (19%)
  local copies, waits for them, and re-layouts  44.7 us (12%)
  between operations  14.6 us (4%)
    psum x1, waiting for transfers between devices, body(): lax.psum((local_kernel, local_noise), ('inner', 'outer'))  77.7 us
    psum x1, blocking collectives, body(): lax.psum((local_kernel, local_noise), ('inner', 'outer'))  38.7 us
    dynamic_slice x48, local copies, waits for them, and re-layouts, body(): lax.scan(summarize, (unit, nothing), (blocks, derivative_results), revers...  33.9 us
    all_gather x3, blocking collectives, entering(): pieces = jax.tree.map(lambda part: lax.all_gather(part, axis), value)  32.6 us
    dot_general x24, matrix products, summarize(): new_mat = jnp.dot(wide.T, carry[0], precision=lax.Precision.HIGHEST)  30.3 us
    all_gather x1, waiting for transfers between devices, entering(): pieces = jax.tree.map(lambda part: lax.all_gather(part, axis), value)  29.2 us
    psum x1, waiting for transfers between devices, spread(): return lax.psum(block, axis)  26.5 us
    dot_general x24, matrix products, summarize(): jnp.dot(grad_row + carry[1], wide, precision=lax.Precision.HIGHEST)  24.9 us
  transfers between devices with their start and end apart: 3, of which 3 were waited for; matrix products, arithmetic and copies ran while one was open for 0% of the time, Pallas kernels for 0%

commit v1 on v0

--- a/solution.py
+++ b/solution.py
@@ -22,7 +22,7 @@
 
 def spread(block, axis, source):
     block = jnp.where(lax.axis_index(axis) == source, block, jnp.zeros_like(block))
-    return lax.psum(block, axis)
+    return jnp.sum(lax.all_gather(block, axis), axis=0)
 
 
 def compose(earlier, later):

time: 374 us -> 356 us (0.952)
  waiting for transfers between devices: 133 us -> 108 us
  blocking collectives: 71.3 us -> 80.7 us
    psum x1 -> x0, waiting for transfers between devices: 26.5 us -> none  [spread(): return lax.psum(block, axis)]
    all_gather x0 -> x1, blocking collectives: none -> 5.99 us  [spread(): return jnp.sum(lax.all_gather(block, axis), axis=0)]
  transfers between devices with their start and end apart: 3 -> 2, of which waited for: 3 -> 2; matrix products, arithmetic and copies ran while one was open for 0% -> 0% of each run, Pallas kernels for 0% -> 0%
where the time goes in v1:
time: 356 us; the launch traced here: 352 us
  waiting for transfers between devices  108 us (30%)
  matrix products  101 us (28%)
  blocking collectives  80.7 us (23%)
  local copies, waits for them, and re-layouts  43 us (12%)
  between operations  14.9 us (4%)
    psum x1, waiting for transfers between devices, body(): lax.psum((local_kernel, local_noise), ('inner', 'outer'))  77.4 us
    psum x1, blocking collectives, body(): lax.psum((local_kernel, local_noise), ('inner', 'outer'))  38.8 us
    all_gather x3, blocking collectives, entering(): pieces = jax.tree.map(lambda part: lax.all_gather(part, axis), value)  35.9 us
    dynamic_slice x48, local copies, waits for them, and re-layouts, body(): lax.scan(summarize, (unit, nothing), (blocks, derivative_results), revers...  33.9 us
    all_gather x1, waiting for transfers between devices, entering(): pieces = jax.tree.map(lambda part: lax.all_gather(part, axis), value)  30.4 us
    dot_general x24, matrix products, summarize(): new_mat = jnp.dot(wide.T, carry[0], precision=lax.Precision.HIGHEST)  30.3 us
    dot_general x24, matrix products, summarize(): jnp.dot(grad_row + carry[1], wide, precision=lax.Precision.HIGHEST)  24.9 us
    dot_general x24, matrix products, backward(): jnp.dot(lam, matrix.astype(jnp.float32), precision=lax.Precision.HIGHEST)  24.9 us
  transfers between devices with their start and end apart: 2, of which 2 were waited for; matrix products, arithmetic and copies ran while one was open for 0% of the time, Pallas kernels for 0%

profile of v1, /device:TPU:1, one launch (start us, length us, event | category | flops | bytes accessed | tf_op | source)
XLA Modules:
  0.0 351.7 jit_solution(10588288045591288427)
XLA Ops:
  7.3 73.5 %while.52 = (s32[]{:T(128)}, f32[256,256]{1,0:T(8,128)S(1)}, f32[256]{0:T(256)S(1)}, bf16[24,256,256]{2,1,0:T(8,128)(2,1)}, f32[24,256]{1,0:T(8,128)}, /*index=5*/s32[]{:T(128)}, s32[]{:T(128)}) while((s32[]{:T(128)}, f32[256,256]{1,0:T(8,128)S(1)}, f32[256]{0:T(256)S(1)}, bf16[24,256,256]{2,1,0:T(8,128)(2,1)}, f32[24,256]{1,0:T(8,128)}, ...), condition=%wide.region_1.2_spmd, body=%wide.region_0.1_spmd.sunk | while | flops 202113280 | bytes 1317989 | solution.py:50
  8.0 1.0 fusion.58
  9.1 1.3 fusion.57
  11.1 1.0 fusion.58
  12.1 1.3 fusion.57
  14.1 1.0 fusion.58
  15.2 1.3 fusion.57
  17.2 1.0 fusion.58
  18.2 1.3 fusion.57
  20.3 1.0 fusion.58
  21.3 1.3 fusion.57
  23.3 1.0 fusion.58
  24.4 1.3 fusion.57
  26.4 1.0 fusion.58
  27.4 1.3 fusion.57
  30.5 1.3 fusion.57
  32.5 1.0 fusion.58
  33.6 1.3 fusion.57
  35.6 1.0 fusion.58
  36.6 1.3 fusion.57
  39.7 1.3 fusion.57
  41.7 1.0 fusion.58
  42.7 1.3 fusion.57
  44.8 1.0 fusion.58
  45.8 1.3 fusion.57
  48.9 1.3 fusion.57
  50.9 1.0 fusion.58
  51.9 1.3 fusion.57
  54.0 1.0 fusion.58
  55.0 1.3 fusion.57
  58.1 1.3 fusion.57
  61.1 1.3 fusion.57
  64.2 1.3 fusion.57
  67.3 1.3 fusion.57
  70.3 1.3 fusion.57
  73.4 1.3 fusion.57
  76.4 1.3 fusion.57
  79.5 1.3 fusion.57
  80.8 3.7 %all-gather.3 = f32[2,1,256]{2,1,0:T(1,128)S(1)} all-gather(f32[1,1,256]{2,1,0:T(1,128)S(1)} %bitcast.109), channel_id=3, replica_groups=mesh['inner'=2,'outer'=16] {'inner'}, dimensions={0}, use_global_device_ids=true | all-gather | bytes 3072 | tf_op jit(solution)/shard_map/all_gather | solution.py:9
  84.5 6.9 %all-gather = f32[512,256]{1,0:T(8,128)S(1)} all-gather(f32[256,256]{1,0:T(8,128)S(1)} %get-tuple-element.325), channel_id=2, replica_groups=mesh['inner'=2,'outer'=16] {'inner'}, dimensions={0}, use_global_device_ids=true | all-gather | bytes 786432 | tf_op jit(solution)/shard_map/all_gather | solution.py:9
  92.8 6.0 %all_gather.29 = f32[2,257,256]{2,1,0:T(8,128)S(1)} all-gather(f32[1,257,256]{2,1,0:T(8,128)S(1)} %maximum_select_fusion), channel_id=1, replica_groups=mesh['inner'=2,'outer'=16] {'inner'}, dimensions={0}, use_global_device_ids=true | all-gather | bytes 789504 | tf_op jit(solution)/shard_map/all_gather | solution.py:25
  99.6 25.3 %all-gather.4 = f32[16,1,256]{2,1,0:T(1,128)S(1)} all-gather(f32[1,1,256]{2,1,0:T(1,128)S(1)} %slice_bitcast_fusion), channel_id=1, replica_groups=mesh['inner'=2,'outer'=16] {'outer'}, dimensions={0}, use_global_device_ids=true | all-gather | bytes 17408 | tf_op jit(solution)/shard_map/all_gather | solution.py:9
  125.0 30.4 %all-gather.7.cloned.1.call-done = f32[4096,256]{1,0:T(8,128)} async-done(((f32[256,256]{1,0:T(8,128)}), f32[4096,256]{1,0:T(8,128)}) %all-gather.7.cloned.1.call-update) | async-done | bytes 4194320 | tf_op jit(solution)/shard_map/all_gather | solution.py:9
  155.4 4.5 %rev.8 = f32[16,256,256]{2,1,0:T(8,128)} reverse(f32[16,256,256]{2,1,0:T(8,128)} %bitcast.95), dimensions={0} | reverse | bytes 8388608 | tf_op jit(solution)/shard_map/rev | solution.py:10
  159.9 20.1 %while.54 = (s32[]{:T(128)}, f32[256]{0:T(256)S(1)}, s32[]{:T(128)}, f32[16,256,256]{2,1,0:T(8,128)}, f32[16,256]{1,0:T(8,128)S(1)}, /*index=5*/s32[]{:T(128)}, s32[]{:T(128)}) while((s32[]{:T(128)}, f32[256]{0:T(256)S(1)}, s32[]{:T(128)}, f32[16,256,256]{2,1,0:T(8,128)}, f32[16,256]{1,0:T(8,128)S(1)}, /*index=5*/s32[]{:T(128)}, ...), condition=%wide.region_4.5_spmd.clone, body=%wide.region_3.4_spmd.clone.sunk | while | flops 787460 | bytes 272498 | solution.py:20
  159.9 1.2 fusion.64
  161.3 1.2 fusion.64
  162.6 1.2 fusion.64
  164.0 1.2 fusion.64
  165.3 1.2 fusion.64
  166.7 1.2 fusion.64
  168.0 1.2 fusion.64
  169.4 1.2 fusion.64
  170.7 1.2 fusion.64
  172.0 1.2 fusion.64
  173.4 1.2 fusion.64
  174.7 1.2 fusion.64
  176.1 1.2 fusion.64
  177.4 1.2 fusion.64
  178.8 1.2 fusion.64
  180.4 44.2 %while.53 = (s32[]{:T(128)}, f32[256]{0:T(256)S(1)}, f32[24,256]{1,0:T(8,128)S(1)}, f32[24,256]{1,0:T(8,128)}, bf16[24,256,256]{2,1,0:T(8,128)(2,1)}, /*index=5*/s32[]{:T(128)}, s32[]{:T(128)}, s32[]{:T(128)}) while((s32[]{:T(128)}, f32[256]{0:T(256)S(1)}, f32[24,256]{1,0:T(8,128)S(1)}, f32[24,256]{1,0:T(8,128)}, ...), condition=%wide.region_6.7_spmd, body=%wide.region_5.6_spmd.sunk | while | flops 786691 | bytes 140397 | solution.py:68
  227.1 38.8 %psum.15 = f32[]{:T(128)} all-reduce(f32[]{:T(128)S(6)} %neg.3), channel_id=1, replica_groups=mesh['inner'=2,'outer'=16] {'inner','outer'}, use_global_device_ids=true, to_apply=%region_9.10 | all-reduce | flops 1 | bytes 8 | tf_op jit(solution)/shard_map/psum | solution.py:77
  265.9 77.4 %all-reduce.2.cloned.1.call-done = f32[128,128]{1,0:T(8,128)} async-done(((f32[128,128]{1,0:T(8,128)}), f32[128,128]{1,0:T(8,128)}) %all-reduce.2.cloned.1.call-update) | async-done | bytes 65552 | tf_op jit(solution)/shard_map/psum | solution.py:77
  343.4 1.5 copy.38
  (257 shorter events, 78.2 us)
Async XLA Ops:
  7.2 148.2 %all-gather.7.cloned.1.call-start = ((), (), s32[]{:S(2)}) async-start(), calls=%async_computation.1 | async-start | bytes 4456448 | tf_op jit(solution)/shard_map/all_gather | solution.py:9
  80.8 44.2 %copy-start.1 = (f32[1,24,2,128]{3,2,1,0:T(2,128)S(1)}, f32[1,24,2,128]{3,2,1,0:T(2,128)}, u32[]{:S(2)}) copy-start(f32[1,24,2,128]{3,2,1,0:T(2,128)} %param.12) | copy-start | bytes 73732
  99.6 243.8 %all-reduce.2.cloned.1.call-start = ((), (), s32[]{:S(2)}) async-start(), calls=%async_computation | async-start | bytes 131072 | tf_op jit(solution)/shard_map/psum | solution.py:77
  155.4 70.5 %copy-start.2 = (f32[1,24,256]{2,1,0:T(8,128)S(1)}, f32[1,24,256]{2,1,0:T(8,128)}, u32[]{:S(2)}) copy-start(f32[1,24,256]{2,1,0:T(8,128)} %param.13) | copy-start | bytes 73732
  224.6 120.2 %copy-start = (f32[24,256]{1,0:T(8,128)}, f32[24,256]{1,0:T(8,128)S(1)}, u32[]{:S(2)}) copy-start(f32[24,256]{1,0:T(8,128)S(1)} %get-tuple-element.328) | copy-start | bytes 73732
Sparse Core Ops, SparseCore 0:
  99.7 55.6 all-gather.6
  226.0 117.3 all-reduce.1
